TPU v7x, 128 devices: a whole 4x4x4 slice. The times are simulated.
128 devices in a mesh: wall: 8 (over z, core), sx: 4 (over x), sy: 4 (over y).
Axes of the slice: x: 4, y: 4, z: 4, core: 2. Of those that a mesh axis runs over, the one named last changes fastest.
Arguments:
- forcing: float32 [4, 8, 32, 384], P('sx', 'sy', 'wall'), may hold values from -17 to 17
- pivot_inverse: float32 [4, 8, 32, 384, 384], P('sx', 'sy', 'wall'), may hold values from -1 to 5
- lower_face: float32 [4, 8, 32, 96, 96], P('sx', 'sy', 'wall'), may hold values from -1 to 2
- upper_face: float32 [4, 8, 32, 96, 96], P('sx', 'sy', 'wall'), may hold values from -1 to 2
- side_coupling: float32 [4, 8, 32, 4, 96, 96], P('sx', 'sy', 'wall'), may hold values from -0.3125 to 0.3125
- orientation: int32 [4, 8, 32, 4], P('sx', 'sy', 'wall'), may hold values from 0 to 3
Outputs:
- solution: float32 [4, 8, 32, 384], P('sx', 'sy', 'wall')
- relative_residual: float32 [], replicated
- forcing_rms: float32 [], replicated
All inputs are finite; a program needn't handle non-finite values.
Results may differ from a plain program's by a relative error of at most 0.0003.
Values sent between devices are 32-bit elements; how exact they have to be, the bound alone decides.
No kernel may reach another device: no remote copies, remote signals or barrier semaphores. Data moves between devices by JAX's collectives and lax.ppermute only.
A program may use at most 64 MiB of HBM per device.

v0:
```python
import jax
import jax.numpy as jnp
from jax import lax
from jax.sharding import PartitionSpec as P

PTS = 4
VARS = 6
BLOCK = 384
FACE = 96
ITERS = 3


precise = lax.Precision.HIGHEST


def entering(part, axis, combine, identity, reverse):
    count = lax.axis_size(axis)
    place = lax.axis_index(axis)
    ahead = count - 1 - place if reverse else place
    gathered = jax.tree.map(lambda a: lax.all_gather(a, axis), part)
    state = jax.tree.map(lambda a, e: jnp.zeros_like(a) + jnp.asarray(e, a.dtype), part, identity)

    def one(step, state):
        source = count - 1 - step if reverse else step
        return combine(
            state, jax.tree.map(lambda a: lax.dynamic_index_in_dim(a, source, 0, False), gathered)
        )

    return lax.fori_loop(0, ahead, one, state)


def extended(block, sides, width):
    for axis, dim in sides:
        count = lax.axis_size(axis)
        forward = [(i, i + 1) for i in range(count - 1)]
        backward = [(target, source) for source, target in forward]
        low = lax.ppermute(
            lax.slice_in_dim(block, block.shape[dim] - width, None, axis=dim), axis, forward
        )
        high = lax.ppermute(lax.slice_in_dim(block, 0, width, axis=dim), axis, backward)
        block = jnp.concatenate([low, block, high], axis=dim)
    return block


def face_traces(vector_in):
    leading = vector_in.shape[:-1]
    node_grid = vector_in.reshape(leading + (PTS, PTS, PTS, VARS))
    facets = [
        node_grid[..., :, :, 0, :],
        node_grid[..., :, :, PTS - 1, :],
        node_grid[..., :, 0, :, :],
        node_grid[..., :, PTS - 1, :, :],
    ]
    flattened = [one_facet.reshape(leading + (FACE,)) for one_facet in facets]
    return jnp.stack(flattened, -2).reshape(leading + (4 * FACE,))


def lateral_term(vector_in, padded, side_coupling, orientation):
    single_row_block, rows_two = (vector_in.shape[0], vector_in.shape[1])
    beside_all = padded.reshape(padded.shape[:3] + (4, FACE))
    across = jnp.stack(
        [
            beside_all[0:single_row_block, 1 : rows_two + 1, :, 1],
            beside_all[2 : single_row_block + 2, 1 : rows_two + 1, :, 0],
            beside_all[1 : single_row_block + 1, 0:rows_two, :, 3],
            beside_all[1 : single_row_block + 1, 2 : rows_two + 2, :, 2],
        ],
        3,
    )
    shaped = across.reshape(across.shape[:4] + (PTS, PTS, VARS))
    turned = jnp.zeros(shaped.shape, jnp.float32)
    for quarter in range(4):
        picked = (orientation == quarter).astype(jnp.float32)[..., None, None, None]
        turned = turned + picked * jnp.rot90(shaped, quarter, axes=(4, 5))
    coupled = jnp.einsum(
        "xyefab,xyefb->xyefa", side_coupling, turned.reshape(across.shape), precision=precise
    )
    pieces = coupled.reshape(across.shape[:4] + (PTS, PTS, VARS))
    result = jnp.zeros(vector_in.shape[:3] + (PTS, PTS, PTS, VARS), jnp.float32)
    result = result.at[:, :, :, :, :, 0, :].add(pieces[:, :, :, 0])
    result = result.at[:, :, :, :, :, PTS - 1, :].add(pieces[:, :, :, 1])
    result = result.at[:, :, :, :, 0, :, :].add(pieces[:, :, :, 2])
    result = result.at[:, :, :, :, PTS - 1, :, :].add(pieces[:, :, :, 3])
    return result.reshape(vector_in.shape)


def apply_map(matrix, vector):
    return jnp.einsum("xyab,xyb->xya", matrix, vector, precision=precise)


def compose(earlier, later):
    return (
        jnp.einsum("xyab,xybc->xyac", later[0], earlier[0], precision=precise),
        apply_map(later[0], earlier[1]) + later[1],
    )


def pass_lower(outgoing, lower_total, identity):
    mapped = entering(
        (lower_total, outgoing), "wall", compose, (identity, jnp.zeros_like(outgoing)), False
    )
    return mapped[1]


def pass_upper(outgoing, upper_total, identity):
    mapped = entering(
        (upper_total, outgoing), "wall", compose, (identity, jnp.zeros_like(outgoing)), True
    )
    return mapped[1]


def solve_small(matrix, vector):
    extent = matrix.shape[0]
    index_ids = jnp.arange(extent)
    for k in range(extent):
        factor_col = jnp.where(index_ids > k, matrix[:, k] / matrix[k, k], 0.0)
        matrix = matrix - factor_col[:, None] * matrix[k][None, :]
        vector = vector - factor_col * vector[k]
    solved = jnp.zeros((extent,), jnp.float32)
    for k in reversed(range(extent)):
        solved = solved.at[k].set((vector[k] - jnp.sum(matrix[k] * solved)) / matrix[k, k])
    return solved


def least_squares(hessenberg, initial_norm):
    target = jnp.zeros((hessenberg.shape[0],), jnp.float32).at[0].set(initial_norm)
    normal = jnp.dot(hessenberg.T, hessenberg, precision=precise)
    weights = solve_small(normal, jnp.dot(hessenberg.T, target, precision=precise))
    misfit = target - jnp.dot(hessenberg, weights, precision=precise)
    return (weights, jnp.sqrt(jnp.sum(misfit * misfit)) / initial_norm)


def shards(forcing, pivot_inverse, lower_face, upper_face, side_coupling, orientation):
    elements = forcing.shape[2]
    lower_maps = -jnp.einsum(
        "xyeab,xyebc->xyeac",
        pivot_inverse[..., BLOCK - FACE :, :FACE],
        lower_face,
        precision=precise,
    )
    upper_maps = -jnp.einsum(
        "xyeab,xyebc->xyeac",
        pivot_inverse[..., :FACE, BLOCK - FACE :],
        upper_face,
        precision=precise,
    )
    identity = jnp.broadcast_to(jnp.eye(FACE, dtype=jnp.float32), forcing.shape[:2] + (FACE, FACE))
    lower_total = identity
    for i in range(elements):
        lower_total = jnp.einsum(
            "xyab,xybc->xyac", lower_maps[:, :, i], lower_total, precision=precise
        )
    upper_total = identity
    for i in reversed(range(elements)):
        upper_total = jnp.einsum(
            "xyab,xybc->xyac", upper_maps[:, :, i], upper_total, precision=precise
        )
    squares = lax.psum(jnp.sum(forcing * forcing), ("wall", "sx", "sy"))
    entry_count = forcing.size * lax.axis_size("wall") * lax.axis_size("sx") * lax.axis_size("sy")
    forcing_rms = jnp.sqrt(squares / entry_count)
    initial_norm = jnp.sqrt(squares)
    krylov = [forcing / initial_norm]
    directions = []
    columns = []
    for j in range(ITERS):
        resid = krylov[j]
        ahead_part = jnp.einsum(
            "xyeab,xyeb->xyea", pivot_inverse[..., BLOCK - FACE :, :], resid, precision=precise
        )
        carried = jnp.zeros(resid.shape[:2] + (FACE,), jnp.float32)
        for precondition_i in range(elements):
            carried = ahead_part[:, :, precondition_i] + apply_map(
                lower_maps[:, :, precondition_i], carried
            )
        carried = pass_lower(carried, lower_total, identity)
        rows_out = []
        for precondition_i in range(elements):
            lowered = apply_map(lower_face[:, :, precondition_i], carried)
            rows_out.append(
                jnp.concatenate(
                    [
                        resid[:, :, precondition_i, :FACE] - lowered,
                        resid[:, :, precondition_i, FACE:],
                    ],
                    -1,
                )
            )
            carried = ahead_part[:, :, precondition_i] + apply_map(
                lower_maps[:, :, precondition_i], carried
            )
        reduced = jnp.stack(rows_out, 2)
        trailing_rows = jnp.einsum(
            "xyeab,xyeb->xyea", pivot_inverse[..., :FACE, :], reduced, precision=precise
        )
        carried = jnp.zeros(resid.shape[:2] + (FACE,), jnp.float32)
        for precondition_i in reversed(range(elements)):
            carried = trailing_rows[:, :, precondition_i] + apply_map(
                upper_maps[:, :, precondition_i], carried
            )
        carried = pass_upper(carried, upper_total, identity)
        rows_back = [None] * elements
        for precondition_i in reversed(range(elements)):
            raised = apply_map(upper_face[:, :, precondition_i], carried)
            rows_back[precondition_i] = jnp.concatenate(
                [
                    reduced[:, :, precondition_i, : BLOCK - FACE],
                    reduced[:, :, precondition_i, BLOCK - FACE :] - raised,
                ],
                -1,
            )
            carried = trailing_rows[:, :, precondition_i] + apply_map(
                upper_maps[:, :, precondition_i], carried
            )
        direction = jnp.einsum(
            "xyeab,xyeb->xyea", pivot_inverse, jnp.stack(rows_back, 2), precision=precise
        )
        directions.append(direction)
        traces = face_traces(direction)
        padded = extended(traces, (("sx", 0), ("sy", 1)), 1)
        vector_w = krylov[j] + lateral_term(direction, padded, side_coupling, orientation)
        listed = []
        for i in range(j + 1):
            projected = lax.psum(jnp.sum(vector_w * krylov[i]), ("wall", "sx", "sy"))
            vector_w = vector_w - projected * krylov[i]
            listed.append(projected)
        coeffs = jnp.stack(listed)
        length = jnp.sqrt(lax.psum(jnp.sum(vector_w * vector_w), ("wall", "sx", "sy")))
        krylov.append(vector_w / length)
        columns.append(
            jnp.concatenate([coeffs, length[None], jnp.zeros((ITERS - 1 - j,), jnp.float32)])
        )
    hessenberg = jnp.stack(columns, 1)
    weights, relative = least_squares(hessenberg, initial_norm)
    solution = weights[0] * directions[0]
    for j in range(1, ITERS):
        solution = solution + weights[j] * directions[j]
    return (solution, relative, forcing_rms)


def solution(mesh):
    return jax.shard_map(
        shards,
        mesh=mesh,
        in_specs=(
            P("sx", "sy", "wall", None),
            P("sx", "sy", "wall", None, None),
            P("sx", "sy", "wall", None, None),
            P("sx", "sy", "wall", None, None),
            P("sx", "sy", "wall", None, None, None),
            P("sx", "sy", "wall", None),
        ),
        out_specs=(P("sx", "sy", "wall", None), P(), P()),
        check_vma=False,
    )
```

profile of v0, /device:TPU:0, one launch (start us, length us, event | category | flops | bytes accessed | tf_op | source)
XLA Modules:
  0.0 1070.7 jit_solution(2524198572940885044)
XLA Ops:
  2.1 68.2 %psum.70 = f32[]{:T(128)} all-reduce(f32[]{:T(128)} %multiply_reduce_fusion.9), channel_id=1, replica_groups=mesh['wall'=8,'sx'=4,'sy'=4] {'wall','sx','sy'}, use_global_device_ids=true, to_apply=%region_1.0 | all-reduce | flops 1 | bytes 8 | tf_op jit(solution)/shard_map/psum | solution.py:158
  73.7 1.6 fusion.43
  75.4 2.6 fusion.54
  79.1 8.4 all-gather.8
  88.5 13.4 %all-gather = f32[16,96,96]{2,1,0:T(8,128)S(1)} all-gather(f32[2,96,96]{2,1,0:T(8,128)S(1)} %fusion.152), channel_id=2, replica_groups=mesh['wall'=8,'sx'=4,'sy'=4] {'wall'}, dimensions={0}, use_global_device_ids=true | all-gather | bytes 663552 | tf_op jit(solution)/shard_map/all_gather | solution.py:20
  105.8 1.7 fusion.42
  109.0 1.7 fusion.166
  115.9 2.6 fusion.48
  120.1 11.7 %all-gather.9 = f32[8,2,96]{2,1,0:T(2,128)} all-gather(f32[1,2,96]{2,1,0:T(2,128)S(1)} %fusion.257), channel_id=5, replica_groups=mesh['wall'=8,'sx'=4,'sy'=4] {'wall'}, dimensions={0}, use_global_device_ids=true | all-gather | bytes 6912 | tf_op jit(solution)/shard_map/all_gather | solution.py:20
  133.3 14.5 %all-gather.2 = f32[16,96,96]{2,1,0:T(8,128)} all-gather(f32[2,96,96]{2,1,0:T(8,128)S(1)} %fusion.156), channel_id=4, replica_groups=mesh['wall'=8,'sx'=4,'sy'=4] {'wall'}, dimensions={0}, use_global_device_ids=true | all-gather | bytes 663552 | tf_op jit(solution)/shard_map/all_gather | solution.py:20
  147.8 13.0 %while.95 = (s32[]{:T(128)}, f32[1,2,96]{2,1,0:T(2,128)S(1)}, s32[]{:T(128)}, f32[8,1,2,96,96]{4,3,2,1,0:T(8,128)}, f32[8,1,2,96]{3,2,1,0:T(2,128)}, /*index=5*/s32[]{:T(128)}, s32[]{:T(128)}, s32[]{:T(128)}, s32[]{:T(128)}) while((s32[]{:T(128)}, f32[1,2,96]{2,1,0:T(2,128)S(1)}, s32[]{:T(128)}, f32[8,1,2,96,96]{4,3,2,1,0:T(8,128)}, ...), condition=%wide.region_5.6_spmd, body=%wide.region_4.5_spmd.sunk | while | flops 221382 | bytes 102291 | solution.py:29
  169.1 6.6 fusion.34
  180.0 2.2 collective-permute-start
  183.6 4.2 collective-permute-done.1
  187.8 2.1 collective-permute-start.2
  192.0 3.6 collective-permute-done.3
  201.4 3.3 fusion.40
  205.4 1.8 reshape.1570
  209.5 2.8 scatter-add.41
  213.8 1.7 copy.239
  217.1 1.8 reshape.1573
  218.9 2.0 multiply_reduce_fusion.8
  220.9 62.9 %psum.71 = f32[]{:T(128)} all-reduce(f32[]{:T(128)} %get-tuple-element.783), channel_id=1, replica_groups=mesh['wall'=8,'sx'=4,'sy'=4] {'wall','sx','sy'}, use_global_device_ids=true, to_apply=%region_7.8 | all-reduce | flops 1 | bytes 8 | tf_op jit(solution)/shard_map/psum | solution.py:223
  283.8 2.0 multiply_reduce_fusion.7
  285.8 62.9 %psum.72 = f32[]{:T(128)} all-reduce(f32[]{:T(128)} %multiply_reduce_fusion.7), channel_id=1, replica_groups=mesh['wall'=8,'sx'=4,'sy'=4] {'wall','sx','sy'}, use_global_device_ids=true, to_apply=%region_9.10 | all-reduce | flops 1 | bytes 8 | tf_op jit(solution)/shard_map/psum | solution.py:227
  351.9 2.6 fusion.52
  356.0 10.9 %all-gather.10 = f32[8,2,96]{2,1,0:T(2,128)} all-gather(f32[1,2,96]{2,1,0:T(2,128)S(1)} %fusion.252), channel_id=6, replica_groups=mesh['wall'=8,'sx'=4,'sy'=4] {'wall'}, dimensions={0}, use_global_device_ids=true | all-gather | bytes 6912 | tf_op jit(solution)/shard_map/all_gather | solution.py:20
  382.5 2.6 fusion.46
  386.6 21.7 %all-gather.11 = f32[8,2,96]{2,1,0:T(2,128)} all-gather(f32[1,2,96]{2,1,0:T(2,128)S(1)} %fusion.248), channel_id=7, replica_groups=mesh['wall'=8,'sx'=4,'sy'=4] {'wall'}, dimensions={0}, use_global_device_ids=true | all-gather | bytes 6912 | tf_op jit(solution)/shard_map/all_gather | solution.py:20
  408.9 16.8 %while.97 = (s32[]{:T(128)}, f32[1,2,96]{2,1,0:T(2,128)}, s32[]{:T(128)}, f32[8,1,2,96,96]{4,3,2,1,0:T(8,128)}, f32[8,1,2,96]{3,2,1,0:T(2,128)}, /*index=5*/s32[]{:T(128)}, s32[]{:T(128)}, s32[]{:T(128)}, s32[]{:T(128)}) while((s32[]{:T(128)}, f32[1,2,96]{2,1,0:T(2,128)}, s32[]{:T(128)}, f32[8,1,2,96,96]{4,3,2,1,0:T(8,128)}, ...), condition=%wide.region_13.14_spmd, body=%wide.region_12.13_spmd.sunk | while | flops 221382 | bytes 102547 | solution.py:29
  437.0 6.6 fusion.32
  447.8 3.5 collective-permute-start.4
  452.8 4.2 collective-permute-done.5
  459.9 4.2 collective-permute-done.7
  468.6 1.8 reshape.1732
  470.4 3.3 fusion.38
  474.3 1.8 reshape.1584
  478.4 2.8 scatter-add.49
  482.7 1.7 copy.262
  486.0 1.8 reshape.1587
  487.8 2.0 multiply_reduce_fusion.6
  489.8 62.1 %psum.73 = f32[]{:T(128)} all-reduce(f32[]{:T(128)} %get-tuple-element.781), channel_id=1, replica_groups=mesh['wall'=8,'sx'=4,'sy'=4] {'wall','sx','sy'}, use_global_device_ids=true, to_apply=%region_15.16 | all-reduce | flops 1 | bytes 8 | tf_op jit(solution)/shard_map/psum | solution.py:223
  551.9 2.0 multiply_reduce_fusion.5
  553.9 64.1 %psum.74 = f32[]{:T(128)} all-reduce(f32[]{:T(128)} %multiply_reduce_fusion.5), channel_id=1, replica_groups=mesh['wall'=8,'sx'=4,'sy'=4] {'wall','sx','sy'}, use_global_device_ids=true, to_apply=%region_17.18 | all-reduce | flops 1 | bytes 8 | tf_op jit(solution)/shard_map/psum | solution.py:223
  618.0 3.2 multiply_reduce_fusion.4
  621.2 62.2 %psum.75 = f32[]{:T(128)} all-reduce(f32[]{:T(128)} %get-tuple-element.779), channel_id=1, replica_groups=mesh['wall'=8,'sx'=4,'sy'=4] {'wall','sx','sy'}, use_global_device_ids=true, to_apply=%region_19.20 | all-reduce | flops 1 | bytes 8 | tf_op jit(solution)/shard_map/psum | solution.py:227
  686.9 2.6 fusion.50
  691.0 11.2 %all-gather.12 = f32[8,2,96]{2,1,0:T(2,128)} all-gather(f32[1,2,96]{2,1,0:T(2,128)S(1)} %fusion.243), channel_id=8, replica_groups=mesh['wall'=8,'sx'=4,'sy'=4] {'wall'}, dimensions={0}, use_global_device_ids=true | all-gather | bytes 6912 | tf_op jit(solution)/shard_map/all_gather | solution.py:20
  713.5 2.6 fusion.44
  717.6 20.1 %all-gather.13 = f32[8,2,96]{2,1,0:T(2,128)S(1)} all-gather(f32[1,2,96]{2,1,0:T(2,128)S(1)} %fusion.239), channel_id=9, replica_groups=mesh['wall'=8,'sx'=4,'sy'=4] {'wall'}, dimensions={0}, use_global_device_ids=true | all-gather | bytes 6912 | tf_op jit(solution)/shard_map/all_gather | solution.py:20
  737.8 8.4 while.99
  752.3 6.6 fusion.30
  760.3 3.3 collective-permute-start.8
  765.1 4.2 collective-permute-done.9
  772.7 3.7 collective-permute-done.11
  778.2 2.5 fusion.36
  783.7 62.1 %psum.76 = f32[]{:T(128)} all-reduce(f32[]{:T(128)} %get-tuple-element.777), channel_id=1, replica_groups=mesh['wall'=8,'sx'=4,'sy'=4] {'wall','sx','sy'}, use_global_device_ids=true, to_apply=%region_25.26 | all-reduce | flops 1 | bytes 8 | tf_op jit(solution)/shard_map/psum | solution.py:223
  847.1 64.9 %psum.77 = f32[]{:T(128)} all-reduce(f32[]{:T(128)} %multiply_reduce_fusion.2), channel_id=1, replica_groups=mesh['wall'=8,'sx'=4,'sy'=4] {'wall','sx','sy'}, use_global_device_ids=true, to_apply=%region_27.28 | all-reduce | flops 1 | bytes 8 | tf_op jit(solution)/shard_map/psum | solution.py:223
  912.0 2.0 multiply_reduce_fusion.1
  914.7 62.0 %psum.78 = f32[]{:T(128)} all-reduce(f32[]{:T(128)} %multiply_reduce_fusion.1), channel_id=1, replica_groups=mesh['wall'=8,'sx'=4,'sy'=4] {'wall','sx','sy'}, use_global_device_ids=true, to_apply=%region_29.30 | all-reduce | flops 1 | bytes 8 | tf_op jit(solution)/shard_map/psum | solution.py:223
  976.7 2.5 multiply_reduce_fusion
  980.5 64.6 %psum.79 = f32[]{:T(128)} all-reduce(f32[]{:T(128)} %multiply_reduce_fusion), channel_id=1, replica_groups=mesh['wall'=8,'sx'=4,'sy'=4] {'wall','sx','sy'}, use_global_device_ids=true, to_apply=%region_31.32 | all-reduce | flops 1 | bytes 8 | tf_op jit(solution)/shard_map/psum | solution.py:227
  1045.7 2.0 maximum_bitcast_fusion.35
  1066.0 1.9 add_bitcast_fusion
  (478 shorter events, 185.9 us)
Async XLA Ops:
  0.6 200.8 %copy-start = (f32[1,2,4,4,96,96]{5,4,3,2,1,0:T(8,128)S(1)}, f32[1,2,4,4,96,96]{5,4,3,2,1,0:T(8,128)}, u32[]{:S(2)}) copy-start(f32[1,2,4,4,96,96]{5,4,3,2,1,0:T(8,128)} %param.54) | copy-start | bytes 3538948
  0.6 102.7 %copy-start.1 = (f32[1,2,4,96,96]{4,3,2,1,0:T(8,128)S(1)}, f32[1,2,4,96,96]{4,3,2,1,0:T(8,128)}, u32[]{:S(2)}) copy-start(f32[1,2,4,96,96]{4,3,2,1,0:T(8,128)} %param.52) | copy-start | bytes 884740
  0.7 104.3 %copy-start.9 = (f32[96,96]{1,0:T(8,128)}, f32[96,96]{1,0:T(8,128)S(1)}, u32[]{:S(2)}) copy-start(f32[96,96]{1,0:T(8,128)S(1)} %fusion.209) | copy-start | bytes 110596
  78.0 9.6 copy-start.30
  78.2 9.3 copy-start.29
  111.6 53.7 %copy-start.3 = (f32[1,2,4,96,96]{4,3,2,1,0:T(8,128)S(1)}, f32[1,2,4,96,96]{4,3,2,1,0:T(8,128)}, u32[]{:S(2)}) copy-start(f32[1,2,4,96,96]{4,3,2,1,0:T(8,128)} %param.53) | copy-start | bytes 884740
  112.4 3.4 copy-start.23
  118.5 29.3 %copy-start.25 = (f32[2,4,1,96]{3,0,1,2:T(2,128)}, f32[2,4,1,96]{3,0,1,2:T(2,128)S(1)}, u32[]{:S(2)}) copy-start(f32[2,4,1,96]{3,0,1,2:T(2,128)S(1)} %copy.514) | copy-start | bytes 9220
  175.7 0.6 copy-start.10
  178.7 40.2 %copy-start.5 = (f32[1,2,4,384]{3,2,1,0:T(4,128)S(1)}, f32[1,2,4,384]{3,2,1,0:T(4,128)}, u32[]{:S(2)}) copy-start(f32[1,2,4,384]{3,2,1,0:T(4,128)} %param.50) | copy-start | bytes 36868
  180.0 3.6 collective-permute-start
  182.2 5.6 collective-permute-start.1
  187.8 4.1 collective-permute-start.2
  190.0 5.7 collective-permute-start.3
  192.0 9.5 copy-start.14
  192.0 9.5 copy-start.16
  192.0 9.5 copy-start.18
  201.4 227.1 %copy-start.4 = (f32[1,2,4,96,96]{4,3,2,1,0:T(8,128)S(1)}, f32[1,2,4,96,96]{4,3,2,1,0:T(8,128)}, u32[]{:S(2)}) copy-start(f32[1,2,4,96,96]{4,3,2,1,0:T(8,128)} %param.53) | copy-start | bytes 884740
  350.6 1.3 copy-start.6
  354.5 1.5 copy-start.28
  379.1 2.7 copy-start.24
  379.8 2.1 copy-start.22
  381.1 0.7 copy-start.21
  381.9 0.6 copy-start.20
  385.1 1.5 copy-start.27
  443.6 0.6 copy-start.12
  447.8 4.9 collective-permute-start.4
  451.4 5.6 collective-permute-start.5
  457.0 2.9 collective-permute-start.6
  458.4 5.7 collective-permute-start.7
  467.8 234.8 %copy-start.2 = (f32[1,2,4,96,96]{4,3,2,1,0:T(8,128)S(1)}, f32[1,2,4,96,96]{4,3,2,1,0:T(8,128)}, u32[]{:S(2)}) copy-start(f32[1,2,4,96,96]{4,3,2,1,0:T(8,128)} %param.52) | copy-start | bytes 884740
  689.5 1.5 copy-start.26
  746.2 31.4 %copy-start.15 = (f32[2,4,4]{2,1,0:T(4,128)S(1)}, f32[2,4,4]{2,1,0:T(4,128)}, u32[]{:S(2)}) copy-start(f32[2,4,4]{2,1,0:T(4,128)} %copy-done.14) | copy-start | bytes 388
  746.2 31.4 %copy-start.17 = (f32[2,4,4]{2,1,0:T(4,128)S(1)}, f32[2,4,4]{2,1,0:T(4,128)}, u32[]{:S(2)}) copy-start(f32[2,4,4]{2,1,0:T(4,128)} %copy-done.16) | copy-start | bytes 388
  746.2 31.4 %copy-start.19 = (f32[2,4,4]{2,1,0:T(4,128)S(1)}, f32[2,4,4]{2,1,0:T(4,128)}, u32[]{:S(2)}) copy-start(f32[2,4,4]{2,1,0:T(4,128)} %copy-done.18) | copy-start | bytes 388
  759.3 23.8 %copy-start.8 = (f32[1,2,4,384]{3,2,1,0:T(4,128)S(1)}, f32[1,2,4,384]{3,2,1,0:T(4,128)}, u32[]{:S(2)}) copy-start(f32[1,2,4,384]{3,2,1,0:T(4,128)} %get-tuple-element.780) | copy-start | bytes 36868
  759.3 86.5 %copy-start.7 = (f32[1,1,8,384]{3,2,1,0:T(8,128)S(1)}, f32[1,1,8,384]{3,2,1,0:T(8,128)}, u32[]{:S(2)}) copy-start(f32[1,1,8,384]{3,2,1,0:T(8,128)} %copy-done.6) | copy-start | bytes 36868
  759.7 306.3 %copy-start.11 = (f32[2,4,1,384]{3,2,1,0:T(1,128)S(1)}, f32[2,4,1,384]{3,2,1,0:T(1,128)}, u32[]{:S(2)}) copy-start(f32[2,4,1,384]{3,2,1,0:T(1,128)} %copy-done.10) | copy-start | bytes 36868
  759.7 306.3 %copy-start.13 = (f32[2,4,1,384]{3,2,1,0:T(1,128)S(1)}, f32[2,4,1,384]{3,2,1,0:T(1,128)}, u32[]{:S(2)}) copy-start(f32[2,4,1,384]{3,2,1,0:T(1,128)} %copy-done.12) | copy-start | bytes 36868
  760.3 4.7 collective-permute-start.8
  763.7 5.6 collective-permute-start.9
  769.3 3.4 collective-permute-start.10
  770.7 5.7 collective-permute-start.11
where the time goes:
time: 1080 us; the launch traced here: 1070 us
  blocking collectives  748 us (69%)
  matrix products  109 us (10%)
  other arithmetic  87.3 us (8%)
  local copies, waits for them, and re-layouts  65.6 us (6%)
  waiting for transfers between devices  24.3 us (2%)
  starting transfers between devices  21.9 us (2%)
  between operations  14.1 us (1%)
    psum x6, blocking collectives, shards(): projected = lax.psum(jnp.sum(vector_w * krylov[i]), ('wall', 'sx', 'sy'))  378 us
    psum x3, blocking collectives, shards(): lax.psum(jnp.sum(vector_w * vector_w), ('wall', 'sx', 'sy'))  190 us
    all_gather x8, blocking collectives, entering(): gathered = jax.tree.map(lambda a: lax.all_gather(a, axis), part)  112 us
    psum x1, blocking collectives, shards(): squares = lax.psum(jnp.sum(forcing * forcing), ('wall', 'sx', 'sy'))  68.2 us
    dot_general x83, matrix products, apply_map(): return jnp.einsum('xyab,xyb->xya', matrix, vector, precision=precise)  56 us
    ppermute x6, waiting for transfers between devices, extended(): lax.ppermute(lax.slice_in_dim(block, 0, width, axis=dim), axis, backward)  24.1 us
  transfers between devices with their start and end apart: 12, of which 9 were waited for; matrix products, arithmetic and copies ran while one was open for 0% of the time, Pallas kernels for 0%

commit v1 on v0

--- a/solution.py
+++ b/solution.py
@@ -130,6 +130,17 @@
     return (weights, jnp.sqrt(jnp.sum(misfit * misfit)) / initial_norm)
 
 
+def allreduce(values):
+    for axis in ("wall", "sx", "sy"):
+        count = lax.axis_size(axis)
+        step = 1
+        while step < count:
+            pairs = [(i, i ^ step) for i in range(count)]
+            values = values + lax.ppermute(values, axis, pairs)
+            step *= 2
+    return values
+
+
 def shards(forcing, pivot_inverse, lower_face, upper_face, side_coupling, orientation):
     elements = forcing.shape[2]
     lower_maps = -jnp.einsum(
@@ -155,15 +166,7 @@
         upper_total = jnp.einsum(
             "xyab,xybc->xyac", upper_maps[:, :, i], upper_total, precision=precise
         )
-    squares = lax.psum(jnp.sum(forcing * forcing), ("wall", "sx", "sy"))
-    entry_count = forcing.size * lax.axis_size("wall") * lax.axis_size("sx") * lax.axis_size("sy")
-    forcing_rms = jnp.sqrt(squares / entry_count)
-    initial_norm = jnp.sqrt(squares)
-    krylov = [forcing / initial_norm]
-    directions = []
-    columns = []
-    for j in range(ITERS):
-        resid = krylov[j]
+    def precond(resid):
         ahead_part = jnp.einsum(
             "xyeab,xyeb->xyea", pivot_inverse[..., BLOCK - FACE :, :], resid, precision=precise
         )
@@ -211,29 +214,66 @@
             carried = trailing_rows[:, :, precondition_i] + apply_map(
                 upper_maps[:, :, precondition_i], carried
             )
-        direction = jnp.einsum(
+        return jnp.einsum(
             "xyeab,xyeb->xyea", pivot_inverse, jnp.stack(rows_back, 2), precision=precise
         )
-        directions.append(direction)
+
+    def lateral(direction):
         traces = face_traces(direction)
         padded = extended(traces, (("sx", 0), ("sy", 1)), 1)
-        vector_w = krylov[j] + lateral_term(direction, padded, side_coupling, orientation)
+        return lateral_term(direction, padded, side_coupling, orientation)
+
+    def dot(a, b):
+        return jnp.sum(a * b)
+
+    entry_count = forcing.size * lax.axis_size("wall") * lax.axis_size("sx") * lax.axis_size("sy")
+    basis = [forcing]
+    precon = []
+    norms = []
+    gram = {}
+    columns = []
+    squares = None
+    for j in range(ITERS):
+        current = basis[j]
+        pre = precond(current)
+        precon.append(pre)
+        mapped = current + lateral(pre)
+        partial = [dot(current, current)] + [dot(mapped, basis[i]) for i in range(j + 1)]
+        partial += [dot(basis[i], current) for i in range(j)]
+        total = allreduce(jnp.stack(partial))
+        norm_sq = total[0]
+        if j == 0:
+            squares = norm_sq
+        norms.append(jnp.sqrt(norm_sq))
+        for i in range(j):
+            gram[(i, j)] = total[2 + j + i] / (norms[i] * norms[j])
         listed = []
         for i in range(j + 1):
-            projected = lax.psum(jnp.sum(vector_w * krylov[i]), ("wall", "sx", "sy"))
-            vector_w = vector_w - projected * krylov[i]
+            projected = total[1 + i] / (norms[i] * norms[j])
+            for l in range(i):
+                projected = projected - listed[l] * gram[(l, i)]
             listed.append(projected)
-        coeffs = jnp.stack(listed)
-        length = jnp.sqrt(lax.psum(jnp.sum(vector_w * vector_w), ("wall", "sx", "sy")))
-        krylov.append(vector_w / length)
-        columns.append(
-            jnp.concatenate([coeffs, length[None], jnp.zeros((ITERS - 1 - j,), jnp.float32)])
-        )
-    hessenberg = jnp.stack(columns, 1)
+        following = mapped / norms[j]
+        for i in range(j + 1):
+            following = following - (listed[i] / norms[i]) * basis[i]
+        basis.append(following)
+        columns.append(listed)
+    last = allreduce(jnp.stack([dot(basis[ITERS], basis[ITERS])]))
+    norms.append(jnp.sqrt(last[0]))
+    full_columns = []
+    for j in range(ITERS):
+        full_columns.append(
+            jnp.concatenate(
+                [jnp.stack(columns[j]), norms[j + 1][None], jnp.zeros((ITERS - 1 - j,), jnp.float32)]
+            )
+        )
+    hessenberg = jnp.stack(full_columns, 1)
+    forcing_rms = jnp.sqrt(squares / entry_count)
+    initial_norm = jnp.sqrt(squares)
     weights, relative = least_squares(hessenberg, initial_norm)
-    solution = weights[0] * directions[0]
+    solution = (weights[0] / norms[0]) * precon[0]
     for j in range(1, ITERS):
-        solution = solution + weights[j] * directions[j]
+        solution = solution + (weights[j] / norms[j]) * precon[j]
     return (solution, relative, forcing_rms)
 
 

time: 1080 us -> 576 us (0.53)
  blocking collectives: 748 us -> 115 us
  waiting for transfers between devices: 24.3 us -> 109 us
  starting transfers between devices: 21.9 us -> 53.2 us
  between operations: 14.1 us -> 28.6 us
    psum x10 -> x0, blocking collectives: 636 us -> none  [the longest x6 378 us: shards(): projected = lax.psum(jnp.sum(vector_w * krylov[i]), ('wall', 'sx', 'sy'))]
    ppermute x0 -> x28, waiting for transfers between devices: none -> 84.1 us  [allreduce(): values = values + lax.ppermute(values, axis, pairs)]
    ppermute x0 -> x28, starting transfers between devices: none -> 25.2 us  [allreduce(): values = values + lax.ppermute(values, axis, pairs)]
    reduce_sum x10 -> x4, other arithmetic: 18.9 us -> 5.31 us  [dot(): return jnp.sum(a * b)]
  transfers between devices with their start and end apart: 12 -> 40, of which waited for: 9 -> 37; matrix products, arithmetic and copies ran while one was open for 0% -> 0% of each run, Pallas kernels for 0% -> 0%
where the time goes in v1:
time: 576 us; the launch traced here: 566 us
  blocking collectives  115 us (20%)
  matrix products  109 us (19%)
  waiting for transfers between devices  109 us (19%)
  other arithmetic  77.5 us (13%)
  local copies, waits for them, and re-layouts  73 us (13%)
  starting transfers between devices  53.2 us (9%)
  between operations  28.6 us (5%)
    all_gather x8, blocking collectives, entering(): gathered = jax.tree.map(lambda a: lax.all_gather(a, axis), part)  115 us
    ppermute x28, waiting for transfers between devices, allreduce(): values = values + lax.ppermute(values, axis, pairs)  84.1 us
    dot_general x83, matrix products, apply_map(): return jnp.einsum('xyab,xyb->xya', matrix, vector, precision=precise)  56 us
    ppermute x28, starting transfers between devices, allreduce(): values = values + lax.ppermute(values, axis, pairs)  25.2 us
    ppermute x6, waiting for transfers between devices, extended(): lax.ppermute(lax.slice_in_dim(block, 0, width, axis=dim), axis, backward)  24.6 us
    ppermute x6, starting transfers between devices, extended(): lax.ppermute(lax.slice_in_dim(block, block.shape[dim] - width, None, axis...  20 us
    dot_general x3, matrix products, precond(): jnp.einsum('xyeab,xyeb->xyea', pivot_inverse, jnp.stack(rows_back, 2), pr...  19.8 us
    add x21, other arithmetic, compose(): apply_map(later[0], earlier[1]) + later[1]  13.3 us
  transfers between devices with their start and end apart: 40, of which 37 were waited for; matrix products, arithmetic and copies ran while one was open for 0% of the time, Pallas kernels for 0%

profile of v1, /device:TPU:0, one launch (start us, length us, event | category | flops | bytes accessed | tf_op | source)
XLA Modules:
  0.0 566.0 jit_solution(9063043285430482014)
XLA Ops:
  5.3 2.6 fusion.54
  9.1 11.9 %all-gather.8 = f32[8,2,96]{2,1,0:T(2,128)S(1)} all-gather(f32[1,2,96]{2,1,0:T(2,128)S(1)} %fusion.264), channel_id=3, replica_groups=mesh['wall'=8,'sx'=4,'sy'=4] {'wall'}, dimensions={0}, use_global_device_ids=true | all-gather | bytes 6912 | tf_op jit(solution)/shard_map/all_gather | solution.py:20
  22.0 13.5 %all-gather = f32[16,96,96]{2,1,0:T(8,128)S(1)} all-gather(f32[2,96,96]{2,1,0:T(8,128)S(1)} %fusion.152), channel_id=2, replica_groups=mesh['wall'=8,'sx'=4,'sy'=4] {'wall'}, dimensions={0}, use_global_device_ids=true | all-gather | bytes 663552 | tf_op jit(solution)/shard_map/all_gather | solution.py:20
  49.4 2.6 fusion.48
  53.6 10.5 %all-gather.9 = f32[8,2,96]{2,1,0:T(2,128)} all-gather(f32[1,2,96]{2,1,0:T(2,128)S(1)} %fusion.260), channel_id=5, replica_groups=mesh['wall'=8,'sx'=4,'sy'=4] {'wall'}, dimensions={0}, use_global_device_ids=true | all-gather | bytes 6912 | tf_op jit(solution)/shard_map/all_gather | solution.py:20
  65.7 14.5 %all-gather.2 = f32[16,96,96]{2,1,0:T(8,128)} all-gather(f32[2,96,96]{2,1,0:T(8,128)S(1)} %fusion.156), channel_id=4, replica_groups=mesh['wall'=8,'sx'=4,'sy'=4] {'wall'}, dimensions={0}, use_global_device_ids=true | all-gather | bytes 663552 | tf_op jit(solution)/shard_map/all_gather | solution.py:20
  80.2 13.3 %while.95 = (s32[]{:T(128)}, f32[1,2,96]{2,1,0:T(2,128)S(1)}, s32[]{:T(128)}, f32[8,1,2,96,96]{4,3,2,1,0:T(8,128)}, f32[8,1,2,96]{3,2,1,0:T(2,128)}, /*index=5*/s32[]{:T(128)}, s32[]{:T(128)}, s32[]{:T(128)}, s32[]{:T(128)}) while((s32[]{:T(128)}, f32[1,2,96]{2,1,0:T(2,128)S(1)}, s32[]{:T(128)}, f32[8,1,2,96,96]{4,3,2,1,0:T(8,128)}, ...), condition=%wide.region_4.5_spmd, body=%wide.region_3.4_spmd.sunk | while | flops 221382 | bytes 102291 | solution.py:29
  101.9 6.6 %fusion.34 = f32[2,4,1,384]{3,2,1,0:T(1,128)S(1)} fusion(f32[1,2,4,384,384]{4,3,2,1,0:T(8,128)} %param.51, f32[1,2,1,384]{3,0,2,1:T(1,128)S(1)} %maximum_bitcast_fusion.16, f32[1,2,1,384]{3,0,2,1:T(1,128)S(1)} %maximum_bitcast_fusion.15, f32[1,2,1,384]{3,0,2,1:T(1,128)S(1)} %copy.230, f32[1,2,1,384]{3,0,2,1:T(1,128)S(1)} %copy.229), kind=kOutput, calls=%fused_computation.40 | convolution fusion | flops 14164992 | bytes 4743168 | tf_op jit(solution)/shard_map/xyeab,xyeb->xyea/dot_general | solution.py:217
  112.7 3.4 collective-permute-start
  117.5 4.2 collective-permute-done.1
  121.7 3.5 collective-permute-start.2
  127.2 3.6 collective-permute-done.3
  136.7 3.3 fusion.40
  144.7 2.8 scatter-add.41
  160.1 3.5 collective-permute-done.5
  165.0 5.0 collective-permute-done.6
  173.6 2.7 collective-permute-start.8
  176.3 2.3 collective-permute-done.8
  182.2 3.1 collective-permute-start.10
  191.3 2.6 fusion.52
  195.4 8.6 %all-gather.10 = f32[8,2,96]{2,1,0:T(2,128)} all-gather(f32[1,2,96]{2,1,0:T(2,128)S(1)} %fusion.255), channel_id=6, replica_groups=mesh['wall'=8,'sx'=4,'sy'=4] {'wall'}, dimensions={0}, use_global_device_ids=true | all-gather | bytes 6912 | tf_op jit(solution)/shard_map/all_gather | solution.py:20
  219.6 2.6 fusion.46
  223.8 23.9 %all-gather.11 = f32[8,2,96]{2,1,0:T(2,128)} all-gather(f32[1,2,96]{2,1,0:T(2,128)S(1)} %fusion.251), channel_id=7, replica_groups=mesh['wall'=8,'sx'=4,'sy'=4] {'wall'}, dimensions={0}, use_global_device_ids=true | all-gather | bytes 6912 | tf_op jit(solution)/shard_map/all_gather | solution.py:20
  248.2 16.6 %while.97 = (s32[]{:T(128)}, f32[1,2,96]{2,1,0:T(2,128)}, s32[]{:T(128)}, f32[8,1,2,96,96]{4,3,2,1,0:T(8,128)}, f32[8,1,2,96]{3,2,1,0:T(2,128)}, /*index=5*/s32[]{:T(128)}, s32[]{:T(128)}, s32[]{:T(128)}, s32[]{:T(128)}) while((s32[]{:T(128)}, f32[1,2,96]{2,1,0:T(2,128)}, s32[]{:T(128)}, f32[8,1,2,96,96]{4,3,2,1,0:T(8,128)}, ...), condition=%wide.region_10.11_spmd, body=%wide.region_9.10_spmd.sunk | while | flops 221382 | bytes 102547 | solution.py:29
  275.9 6.6 %fusion.32 = f32[2,4,1,384]{3,2,1,0:T(1,128)S(1)} fusion(f32[1,2,4,384,384]{4,3,2,1,0:T(8,128)} %param.51, f32[1,2,1,384]{3,0,2,1:T(1,128)S(1)} %maximum_bitcast_fusion.24, f32[1,2,1,384]{3,0,2,1:T(1,128)S(1)} %maximum_bitcast_fusion.23, f32[1,2,1,384]{3,0,2,1:T(1,128)S(1)} %copy.255, f32[1,2,1,384]{3,0,2,1:T(1,128)S(1)} %copy.254), kind=kOutput, calls=%fused_computation.38 | convolution fusion | flops 14164992 | bytes 4743168 | tf_op jit(solution)/shard_map/xyeab,xyeb->xyea/dot_general | solution.py:217
  286.7 3.4 collective-permute-start.11
  291.5 4.2 collective-permute-done.12
  295.7 3.5 collective-permute-start.13
  300.8 4.1 collective-permute-done.14
  311.3 3.3 fusion.38
  319.3 2.8 scatter-add.49
  330.7 2.6 pad_maximum_fusion.11
  334.4 2.6 fusion.421
  337.0 3.5 collective-permute-done.16
  340.5 2.6 fusion.423
  343.2 5.0 collective-permute-done.17
  349.4 2.3 collective-permute-done.18
  353.0 3.8 collective-permute-done.19
  358.1 2.3 collective-permute-done.20
  361.7 3.7 collective-permute-done.21
  371.3 2.6 fusion.50
  375.4 8.6 %all-gather.12 = f32[8,2,96]{2,1,0:T(2,128)} all-gather(f32[1,2,96]{2,1,0:T(2,128)S(1)} %fusion.246), channel_id=8, replica_groups=mesh['wall'=8,'sx'=4,'sy'=4] {'wall'}, dimensions={0}, use_global_device_ids=true | all-gather | bytes 6912 | tf_op jit(solution)/shard_map/all_gather | solution.py:20
  395.6 2.6 fusion.44
  399.7 23.4 %all-gather.13 = f32[8,2,96]{2,1,0:T(2,128)S(1)} all-gather(f32[1,2,96]{2,1,0:T(2,128)S(1)} %fusion.242), channel_id=9, replica_groups=mesh['wall'=8,'sx'=4,'sy'=4] {'wall'}, dimensions={0}, use_global_device_ids=true | all-gather | bytes 6912 | tf_op jit(solution)/shard_map/all_gather | solution.py:20
  423.1 8.4 %while.99 = (s32[]{:T(128)}, f32[1,2,96]{2,1,0:T(2,128)S(1)}, s32[]{:T(128)}, f32[8,1,2,96,96]{4,3,2,1,0:T(8,128)}, f32[8,1,2,96]{3,2,1,0:T(2,128)S(1)}, /*index=5*/s32[]{:T(128)}, s32[]{:T(128)}, s32[]{:T(128)}, s32[]{:T(128)}) while((s32[]{:T(128)}, f32[1,2,96]{2,1,0:T(2,128)S(1)}, s32[]{:T(128)}, f32[8,1,2,96,96]{4,3,2,1,0:T(8,128)}, ...), condition=%wide.region_18.19_spmd, body=%wide.region_17.18_spmd.sunk | while | flops 221382 | bytes 102291 | solution.py:29
  437.7 6.6 %fusion.30 = f32[2,4,1,384]{3,2,1,0:T(1,128)S(1)} fusion(f32[1,2,4,384,384]{4,3,2,1,0:T(8,128)} %param.51, f32[1,2,1,384]{3,0,2,1:T(1,128)S(1)} %maximum_bitcast_fusion.32, f32[1,2,1,384]{3,0,2,1:T(1,128)S(1)} %maximum_bitcast_fusion.31, f32[1,2,1,384]{3,0,2,1:T(1,128)S(1)} %copy.278, f32[1,2,1,384]{3,0,2,1:T(1,128)S(1)} %copy.277), kind=kOutput, calls=%fused_computation.36 | convolution fusion | flops 14164992 | bytes 4743168 | tf_op jit(solution)/shard_map/xyeab,xyeb->xyea/dot_general | solution.py:217
  445.7 3.1 collective-permute-start.22
  451.5 4.3 collective-permute-done.23
  455.8 3.2 collective-permute-start.24
  460.4 4.2 collective-permute-done.25
  466.5 2.5 fusion.36
  472.0 3.8 stack.240
  477.0 3.5 collective-permute-done.27
  480.5 5.0 collective-permute-done.28
  485.6 3.5 collective-permute-done.29
  489.7 4.4 collective-permute-done.30
  494.2 3.5 collective-permute-done.31
  498.6 4.4 collective-permute-done.32
  512.9 2.3 collective-permute-done.34
  517.2 3.8 collective-permute-done.35
  523.1 2.3 collective-permute-done.36
  528.0 3.2 collective-permute-done.37
  533.3 2.3 collective-permute-done.38
  538.2 3.2 collective-permute-done.39
  (544 shorter events, 236.1 us)
Async XLA Ops:
  0.6 136.1 %copy-start = (f32[1,2,4,4,96,96]{5,4,3,2,1,0:T(8,128)S(1)}, f32[1,2,4,4,96,96]{5,4,3,2,1,0:T(8,128)}, u32[]{:S(2)}) copy-start(f32[1,2,4,4,96,96]{5,4,3,2,1,0:T(8,128)} %param.54) | copy-start | bytes 3538948
  0.6 36.2 %copy-start.1 = (f32[1,2,4,96,96]{4,3,2,1,0:T(8,128)S(1)}, f32[1,2,4,96,96]{4,3,2,1,0:T(8,128)}, u32[]{:S(2)}) copy-start(f32[1,2,4,96,96]{4,3,2,1,0:T(8,128)} %param.52) | copy-start | bytes 884740
  0.7 37.8 %copy-start.8 = (f32[96,96]{1,0:T(8,128)}, f32[96,96]{1,0:T(8,128)S(1)}, u32[]{:S(2)}) copy-start(f32[96,96]{1,0:T(8,128)S(1)} %fusion.209) | copy-start | bytes 110596
  8.0 13.0 %copy-start.31 = (f32[2,96,1]{1,0,2:T(2,128)}, f32[2,96,1]{1,0,2:T(2,128)S(1)}, u32[]{:S(2)}) copy-start(f32[2,96,1]{1,0,2:T(2,128)S(1)} %broadcast.388) | copy-start | bytes 2308
  8.2 12.8 %copy-start.30 = (f32[2,1,96]{2,1,0:T(1,128)}, f32[2,1,96]{2,1,0:T(1,128)S(1)}, u32[]{:S(2)}) copy-start(f32[2,1,96]{2,1,0:T(1,128)S(1)} %fusion.160) | copy-start | bytes 2308
  45.1 52.9 %copy-start.3 = (f32[1,2,4,96,96]{4,3,2,1,0:T(8,128)S(1)}, f32[1,2,4,96,96]{4,3,2,1,0:T(8,128)}, u32[]{:S(2)}) copy-start(f32[1,2,4,96,96]{4,3,2,1,0:T(8,128)} %param.53) | copy-start | bytes 884740
  45.9 3.5 copy-start.24
  52.1 28.1 %copy-start.26 = (f32[2,4,1,96]{3,0,1,2:T(2,128)}, f32[2,4,1,96]{3,0,1,2:T(2,128)S(1)}, u32[]{:S(2)}) copy-start(f32[2,4,1,96]{3,0,1,2:T(2,128)S(1)} %copy.514) | copy-start | bytes 9220
  111.4 42.7 %copy-start.5 = (f32[1,2,4,384]{3,2,1,0:T(4,128)S(1)}, f32[1,2,4,384]{3,2,1,0:T(4,128)}, u32[]{:S(2)}) copy-start(f32[1,2,4,384]{3,2,1,0:T(4,128)} %param.50) | copy-start | bytes 36868
  112.7 4.8 collective-permute-start
  116.1 5.6 collective-permute-start.1
  121.7 5.5 collective-permute-start.2
  125.2 5.7 collective-permute-start.3
  127.2 9.5 %copy-start.15 = (f32[2,4,4]{2,1,0:T(4,128)}, f32[2,4,4]{2,1,0:T(4,128)S(1)}, u32[]{:S(2)}) copy-start(f32[2,4,4]{2,1,0:T(4,128)S(1)} %get-tuple-element.847) | copy-start | bytes 388
  127.2 9.5 %copy-start.17 = (f32[2,4,4]{2,1,0:T(4,128)}, f32[2,4,4]{2,1,0:T(4,128)S(1)}, u32[]{:S(2)}) copy-start(f32[2,4,4]{2,1,0:T(4,128)S(1)} %get-tuple-element.848) | copy-start | bytes 388
  127.2 9.5 %copy-start.19 = (f32[2,4,4]{2,1,0:T(4,128)}, f32[2,4,4]{2,1,0:T(4,128)S(1)}, u32[]{:S(2)}) copy-start(f32[2,4,4]{2,1,0:T(4,128)S(1)} %get-tuple-element.849) | copy-start | bytes 388
  136.7 130.8 %copy-start.4 = (f32[1,2,4,96,96]{4,3,2,1,0:T(8,128)S(1)}, f32[1,2,4,96,96]{4,3,2,1,0:T(8,128)}, u32[]{:S(2)}) copy-start(f32[1,2,4,96,96]{4,3,2,1,0:T(8,128)} %param.53) | copy-start | bytes 884740
  157.5 1.1 collective-permute-start.4
  160.0 3.6 collective-permute-start.5
  165.0 5.1 collective-permute-start.6
  170.1 3.5 collective-permute-start.7
  173.6 5.0 collective-permute-start.8
  178.6 3.5 collective-permute-start.9
  182.2 5.2 collective-permute-start.10
  216.2 2.7 copy-start.25
  217.0 2.0 copy-start.23
  222.3 1.5 copy-start.28
  286.7 4.8 collective-permute-start.11
  290.1 5.6 collective-permute-start.12
  295.7 5.0 collective-permute-start.13
  299.2 5.7 collective-permute-start.14
  308.7 75.9 %copy-start.2 = (f32[1,2,4,96,96]{4,3,2,1,0:T(8,128)S(1)}, f32[1,2,4,96,96]{4,3,2,1,0:T(8,128)}, u32[]{:S(2)}) copy-start(f32[1,2,4,96,96]{4,3,2,1,0:T(8,128)} %param.52) | copy-start | bytes 884740
  333.3 1.1 collective-permute-start.15
  337.0 3.6 collective-permute-start.16
  343.1 5.1 collective-permute-start.17
  348.2 3.5 collective-permute-start.18
  351.7 5.0 collective-permute-start.19
  356.8 3.5 collective-permute-start.20
  360.3 5.0 collective-permute-start.21
  431.6 34.3 %copy-start.16 = (f32[2,4,4]{2,1,0:T(4,128)S(1)}, f32[2,4,4]{2,1,0:T(4,128)}, u32[]{:S(2)}) copy-start(f32[2,4,4]{2,1,0:T(4,128)} %copy-done.15) | copy-start | bytes 388
  431.6 34.3 %copy-start.18 = (f32[2,4,4]{2,1,0:T(4,128)S(1)}, f32[2,4,4]{2,1,0:T(4,128)}, u32[]{:S(2)}) copy-start(f32[2,4,4]{2,1,0:T(4,128)} %copy-done.17) | copy-start | bytes 388
  431.6 34.3 %copy-start.20 = (f32[2,4,4]{2,1,0:T(4,128)S(1)}, f32[2,4,4]{2,1,0:T(4,128)}, u32[]{:S(2)}) copy-start(f32[2,4,4]{2,1,0:T(4,128)} %copy-done.19) | copy-start | bytes 388
  444.7 26.6 %copy-start.7 = (f32[1,1,8,384]{3,2,1,0:T(8,128)S(1)}, f32[1,1,8,384]{3,2,1,0:T(8,128)}, u32[]{:S(2)}) copy-start(f32[1,1,8,384]{3,2,1,0:T(8,128)} %copy-done.6) | copy-start | bytes 36868
  444.7 26.6 %copy-start.10 = (f32[1,1,8,384]{3,2,1,0:T(8,128)S(1)}, f32[1,1,8,384]{3,2,1,0:T(8,128)}, u32[]{:S(2)}) copy-start(f32[1,1,8,384]{3,2,1,0:T(8,128)} %copy-done.9) | copy-start | bytes 36868
  445.1 117.5 %copy-start.12 = (f32[2,4,1,384]{3,2,1,0:T(1,128)S(1)}, f32[2,4,1,384]{3,2,1,0:T(1,128)}, u32[]{:S(2)}) copy-start(f32[2,4,1,384]{3,2,1,0:T(1,128)} %copy-done.11) | copy-start | bytes 36868
  445.1 117.5 %copy-start.14 = (f32[2,4,1,384]{3,2,1,0:T(1,128)S(1)}, f32[2,4,1,384]{3,2,1,0:T(1,128)}, u32[]{:S(2)}) copy-start(f32[2,4,1,384]{3,2,1,0:T(1,128)} %copy-done.13) | copy-start | bytes 36868
  445.7 5.7 %collective-permute-start.22 = (f32[1,2,4,384]{3,2,1,0:T(4,128)S(1)}, f32[1,2,4,384]{3,2,1,0:T(4,128)S(1)}, u32[]{:S(2)}, u32[]{:S(2)}) collective-permute-start(f32[1,2,4,384]{3,2,1,0:T(4,128)S(1)} %reshape.1603), channel_id=1, source_target_pairs={{0,4},{4,8},{8,12},{1,5},{5,9},{9,13},{2,6},{6,10},{10,14},{3,7},{... | collective-permute-start | bytes 36872 | tf_op jit(solution)/shard_map/ppermute | solution.py:37
  450.2 5.6 collective-permute-start.23
  455.8 4.6 collective-permute-start.24
  459.0 5.7 collective-permute-start.25
  475.8 1.1 collective-permute-start.26
  477.0 3.5 collective-permute-start.27
  480.5 5.0 collective-permute-start.28
  485.6 3.5 collective-permute-start.29
  489.1 5.0 collective-permute-start.30
  494.2 3.5 collective-permute-start.31
  497.7 5.3 collective-permute-start.32
  508.8 1.4 collective-permute-start.33
  511.5 3.7 collective-permute-start.34
  515.8 5.2 collective-permute-start.35
  521.7 3.7 collective-permute-start.36
  526.0 5.2 collective-permute-start.37
  531.9 3.7 collective-permute-start.38
  536.2 5.2 collective-permute-start.39
  (8 other events, 8.1 us)
